TPU v7x, 128 devices: a whole 4x4x4 slice. The times are simulated.
128 devices in a mesh: row: 4 (over z_lo, core), col: 8 (over y, z_hi), layer: 4 (over x).
Axes of the slice: x: 4, y: 4, z: 4 (z_hi: 2, z_lo: 2; z = z_hi * 2 + z_lo), core: 2. Of those that a mesh axis runs over, the one named last changes fastest.
Arguments:
- a_tiles: bfloat16 [4, 8, 4, 32, 128, 128], P('row', 'col', 'layer'), may hold values from 0 to 1, as said below
- a_coords: int32 [4, 8, 4, 32, 2], P('row', 'col', 'layer'), may hold values from 0 to 31, as said below
- b_tiles: bfloat16 [4, 8, 4, 32, 128, 128], P('row', 'col', 'layer'), may hold values from 0 to 1, as said below
- b_coords: int32 [4, 8, 4, 32, 2], P('row', 'col', 'layer'), may hold values from 0 to 15, as said below
- out_coords: int32 [4, 8, 4, 16, 2], P('row', 'col', 'layer'), may hold values from 0 to 15, as said below
Outputs:
- flow: float32 [4, 8, 4, 16, 128, 128], P('row', 'col', 'layer')
Inputs may be any that keep to these rules, and one draw needn't show every extreme that they name: `a_tiles`: every entry is positive. `b_tiles`: every entry is positive. `a_coords`: on one device, column 0 takes every value below 32 exactly once; column 1 is below 4. `b_coords`: on one device, column 1 takes every value below 16 exactly twice, with two different values of column 0; column 0 is below 8. `out_coords`: on one device, column 1 takes every value below 16 exactly once; column 0 is below 8.
All inputs are finite; a program needn't handle non-finite values.
Results may differ from a plain program's by a relative error of at most 0.0003.
Values may be sent and summed in bfloat16 or wider, within the bound.
No kernel may reach another device: no remote copies, remote signals or barrier semaphores. Data moves between devices by JAX's collectives and lax.ppermute only.
A program may use at most 192 MiB of HBM per device.

v0:
```python
import jax
import jax.numpy as jnp
from jax import lax
from jax.sharding import PartitionSpec as P

BLK = 4
RB = 4


def local(a_tiles, a_coords, b_tiles, b_coords, out_coords):
    tile_size = a_tiles.shape[-1]
    rows_panel = a_tiles.shape[3]
    col_count = lax.axis_size("col")
    row_count = lax.axis_size("row")
    layer_count = lax.axis_size("layer")
    a_span = BLK
    b_span = BLK * col_count // row_count
    slab_tiles = a_span * col_count
    col_tiles = out_coords.shape[3]
    graph_tiles, graph_coords = (
        lax.all_gather(b_tiles, "row", axis=0, tiled=True),
        lax.all_gather(b_coords, "row", axis=0, tiled=True),
    )
    owner_rows = jnp.arange(row_count, dtype=jnp.int32)[:, None]
    inner_rows = (owner_rows * b_span + graph_coords[:, 0, 0, :, 0]).reshape(-1)
    column_ids = graph_coords[:, 0, 0, :, 1].reshape(-1)
    flat_tiles = graph_tiles.reshape(-1, tile_size, tile_size)
    graph_panel = jnp.zeros((slab_tiles, tile_size, col_tiles, tile_size), jnp.bfloat16)
    graph_panel = graph_panel.at[inner_rows, :, column_ids, :].set(flat_tiles)
    graph_panel = graph_panel.reshape(slab_tiles, tile_size, col_tiles * tile_size)
    own_rows = a_coords[0, 0, 0, :, 0]
    own_inner = a_coords[0, 0, 0, :, 1]
    ordered = jnp.zeros_like(a_tiles[0, 0, 0]).at[own_rows].set(a_tiles[0, 0, 0])
    ordered_inner = jnp.zeros_like(own_inner).at[own_rows].set(own_inner)
    flow_all, inner_all = (
        lax.all_gather(ordered[None], "col", axis=0, tiled=True),
        lax.all_gather(ordered_inner[None], "col", axis=0, tiled=True),
    )
    slab_index = jnp.arange(col_count, dtype=jnp.int32)[:, None] * a_span + inner_all

    def row_block(step_index):
        first_row = step_index * RB
        left_block = lax.dynamic_slice_in_dim(flow_all, first_row, RB, 1)
        index_block = lax.dynamic_slice_in_dim(slab_index, first_row, RB, 1)
        right_block = graph_panel[index_block]
        return jnp.einsum(
            "prxy,pryz->rxz", left_block, right_block, preferred_element_type=jnp.float32
        )

    partial_sum = lax.map(row_block, jnp.arange(rows_panel // RB, dtype=jnp.int32))
    partial_sum = partial_sum.reshape(rows_panel, tile_size, col_tiles * tile_size)
    kept_rows = out_coords[0, 0, 0, :, 0]
    kept_cols = out_coords[0, 0, 0, :, 1]
    summed_rows = lax.psum_scatter(partial_sum, "layer", scatter_dimension=0, tiled=True)
    tile_grid = summed_rows.reshape(b_span, tile_size, col_tiles, tile_size)
    kept_tiles = tile_grid[kept_rows, :, kept_cols, :]
    squared = kept_tiles * kept_tiles
    column_part = jnp.sum(squared, axis=1)
    onehot = (jnp.arange(col_tiles, dtype=jnp.int32)[:, None] == kept_cols[None, :]).astype(
        jnp.float32
    )
    local_mass = jnp.dot(onehot, column_part, precision=lax.Precision.HIGHEST)
    column_total = lax.psum(local_mass, ("row", "layer"))
    factor = jnp.float32(row_count * layer_count * tile_size) / column_total
    flow = squared * factor[kept_cols][:, None, :]
    return flow.reshape(1, 1, 1, col_tiles, tile_size, tile_size)


def solution(mesh):
    in_specs = (
        P("row", "col", "layer", None, None, None),
        P("row", "col", "layer", None, None),
        P("row", "col", "layer", None, None, None),
        P("row", "col", "layer", None, None),
        P("row", "col", "layer", None, None),
    )
    out_specs = P("row", "col", "layer", None, None, None)
    return jax.shard_map(local, mesh=mesh, in_specs=in_specs, out_specs=out_specs, check_vma=False)
```

profile of v0, /device:TPU:0, one launch (start us, length us, event | category | flops | bytes accessed | tf_op | source)
XLA Modules:
  0.0 728.4 jit_solution(13771019656350618229)
XLA Ops:
  6.5 0.7 all-gather.5.cloned.1.call-update
  7.3 0.7 fusion.8
  8.2 3.6 scatter_fusion
  11.8 1.0 copy-done
  12.9 5.3 all_gather.14
  18.5 0.7 slice_bitcast_fusion
  19.2 0.7 scatter_custom_fusion.1
  19.9 1.2 dynamic-slice
  21.7 0.2 dynamic-update-slice
  22.0 13.9 %all-reduce = s32[256]{0:T(256)S(1)} all-reduce(s32[256]{0:T(256)S(1)} %dynamic-update-slice), channel_id=3, replica_groups=mesh['row'=4,'col'=8,'layer'=4] {'col'}, use_global_device_ids=true, to_apply=%add | all-reduce | flops 256 | bytes 2048
  36.0 21.7 %all-gather.5.cloned.1.call-done = bf16[4,1,1,32,128,128]{5,4,3,2,1,0:T(8,128)(2,1)} async-done(((bf16[1,1,1,32,128,128]{5,4,3,2,1,0:T(8,128)(2,1)}), bf16[4,1,1,32,128,128]{5,4,3,2,1,0:T(8,128)(2,1)}) %all-gather.5.cloned.1.call-update) | async-done | bytes 4194320 | tf_op jit(solution)/shard_map/all_gather | solution.py:21
  57.7 6.3 broadcast_in_dim.37
  64.0 21.0 %scatter_fusion.1 = bf16[32,128,16,128]{3,1,2,0:T(8,128)(2,1)} fusion(bf16[32,128,16,128]{3,1,2,0:T(8,128)(2,1)} %broadcast_in_dim.37, s32[128]{0:T(128)S(1)} %fusion.13, bf16[128,128,128]{2,1,0:T(8,128)(2,1)} %bitcast.51), kind=kCustom, calls=%fused_computation.5 | custom fusion | bytes 12583936 | tf_op jit(solution)/shard_map/scatter | solution.py:29
  84.9 22.6 %copy.18 = bf16[32,128,16,128]{1,3,2,0:T(8,128)(2,1)} copy(bf16[32,128,16,128]{3,1,2,0:T(8,128)(2,1)} %scatter_fusion.1) | data formatting | bytes 33554432 | tf_op jit(solution)/shard_map/scatter | solution.py:29
  107.6 22.2 %copy.20 = bf16[32,128,2048]{2,1,0:T(8,128)(2,1)} copy(bf16[32,128,2048]{1,2,0:T(8,128)(2,1)} %bitcast.48) | data formatting | bytes 33554432 | tf_op jit(solution)/shard_map/while | solution.py:50
  129.8 40.7 %all-gather.7.cloned.1.call-done = bf16[256,128,128]{2,1,0:T(8,128)(2,1)} async-done(((bf16[32,128,128]{2,1,0:T(8,128)(2,1)}), bf16[256,128,128]{2,1,0:T(8,128)(2,1)}) %all-gather.7.cloned.1.call-update) | async-done | bytes 8388624 | tf_op jit(solution)/shard_map/all_gather | solution.py:36
  170.5 226.7 %while.10 = (s32[]{:T(128)}, f32[8,4,128,2048]{2,3,1,0:T(8,128)}, s32[8]{0:T(128)S(1)}, bf16[8,32,128,128]{3,2,1,0:T(8,128)(2,1)}, s32[8,32]{1,0:T(8,128)S(1)}, ...) while((s32[]{:T(128)}, f32[8,4,128,2048]{2,3,1,0:T(8,128)}, ...), condition=%wide.region_4.5_spmd, body=%wide.region_3.4_spmd.sunk | while | flops 2147484672 | bytes 55580068 | solution.py:50
  170.5 0.6 dynamic_slice.19
  171.9 13.1 %gather_fusion = bf16[32,128,2048]{2,1,0:T(8,128)(2,1)} fusion(bf16[32,128,2048]{2,1,0:T(8,128)(2,1)} %get-tuple-element.134, s32[1024]{0:T(1024)S(1)} %pad_clamp_fusion.3), kind=kCustom, calls=%fused_computation.clone.1 | custom fusion | bytes 33554560 | tf_op jit(solution)/shard_map/while/body/eval_jaxpr/gather | solution.py:45
  185.0 13.8 %bitcast_dynamic-update-slice_fusion.2 = f32[8,4,128,2048]{2,3,1,0:T(8,128)} fusion(f32[8,4,128,2048]{2,3,1,0:T(8,128)} %get-tuple-element.120, s32[]{:T(128)} %get-tuple-element.119, bf16[8,4,128,2048]{3,2,1,0:T(8,128)(2,1)} %bitcast.47, bf16[8,32,128,128]{3,2,1,0:T(8,128)(2,1)} %get-tuple-element.132, s32[]{:T(128)S(6)} %select_n.95), kind=kOutput, calls=%fused_computation.8.clone.1 | convolution fusion | flops 2147483648 | bytes 22020612 | tf_op jit(solution)/shard_map/while/body/eval_jaxpr/prxy,pryz->rxz/dot_general | solution.py:46
  198.8 0.6 dynamic_slice.19
  200.2 13.1 %gather_fusion = bf16[32,128,2048]{2,1,0:T(8,128)(2,1)} fusion(bf16[32,128,2048]{2,1,0:T(8,128)(2,1)} %get-tuple-element.134, s32[1024]{0:T(1024)S(1)} %pad_clamp_fusion.3), kind=kCustom, calls=%fused_computation.clone.1 | custom fusion | bytes 33554560 | tf_op jit(solution)/shard_map/while/body/eval_jaxpr/gather | solution.py:45
  213.3 13.8 %bitcast_dynamic-update-slice_fusion.2 = f32[8,4,128,2048]{2,3,1,0:T(8,128)} fusion(f32[8,4,128,2048]{2,3,1,0:T(8,128)} %get-tuple-element.120, s32[]{:T(128)} %get-tuple-element.119, bf16[8,4,128,2048]{3,2,1,0:T(8,128)(2,1)} %bitcast.47, bf16[8,32,128,128]{3,2,1,0:T(8,128)(2,1)} %get-tuple-element.132, s32[]{:T(128)S(6)} %select_n.95), kind=kOutput, calls=%fused_computation.8.clone.1 | convolution fusion | flops 2147483648 | bytes 22020612 | tf_op jit(solution)/shard_map/while/body/eval_jaxpr/prxy,pryz->rxz/dot_general | solution.py:46
  227.1 0.6 dynamic_slice.19
  228.5 13.1 %gather_fusion = bf16[32,128,2048]{2,1,0:T(8,128)(2,1)} fusion(bf16[32,128,2048]{2,1,0:T(8,128)(2,1)} %get-tuple-element.134, s32[1024]{0:T(1024)S(1)} %pad_clamp_fusion.3), kind=kCustom, calls=%fused_computation.clone.1 | custom fusion | bytes 33554560 | tf_op jit(solution)/shard_map/while/body/eval_jaxpr/gather | solution.py:45
  241.7 13.8 %bitcast_dynamic-update-slice_fusion.2 = f32[8,4,128,2048]{2,3,1,0:T(8,128)} fusion(f32[8,4,128,2048]{2,3,1,0:T(8,128)} %get-tuple-element.120, s32[]{:T(128)} %get-tuple-element.119, bf16[8,4,128,2048]{3,2,1,0:T(8,128)(2,1)} %bitcast.47, bf16[8,32,128,128]{3,2,1,0:T(8,128)(2,1)} %get-tuple-element.132, s32[]{:T(128)S(6)} %select_n.95), kind=kOutput, calls=%fused_computation.8.clone.1 | convolution fusion | flops 2147483648 | bytes 22020612 | tf_op jit(solution)/shard_map/while/body/eval_jaxpr/prxy,pryz->rxz/dot_general | solution.py:46
  255.5 0.6 dynamic_slice.19
  256.9 13.1 %gather_fusion = bf16[32,128,2048]{2,1,0:T(8,128)(2,1)} fusion(bf16[32,128,2048]{2,1,0:T(8,128)(2,1)} %get-tuple-element.134, s32[1024]{0:T(1024)S(1)} %pad_clamp_fusion.3), kind=kCustom, calls=%fused_computation.clone.1 | custom fusion | bytes 33554560 | tf_op jit(solution)/shard_map/while/body/eval_jaxpr/gather | solution.py:45
  270.0 13.8 %bitcast_dynamic-update-slice_fusion.2 = f32[8,4,128,2048]{2,3,1,0:T(8,128)} fusion(f32[8,4,128,2048]{2,3,1,0:T(8,128)} %get-tuple-element.120, s32[]{:T(128)} %get-tuple-element.119, bf16[8,4,128,2048]{3,2,1,0:T(8,128)(2,1)} %bitcast.47, bf16[8,32,128,128]{3,2,1,0:T(8,128)(2,1)} %get-tuple-element.132, s32[]{:T(128)S(6)} %select_n.95), kind=kOutput, calls=%fused_computation.8.clone.1 | convolution fusion | flops 2147483648 | bytes 22020612 | tf_op jit(solution)/shard_map/while/body/eval_jaxpr/prxy,pryz->rxz/dot_general | solution.py:46
  283.8 0.6 dynamic_slice.19
  285.2 13.1 %gather_fusion = bf16[32,128,2048]{2,1,0:T(8,128)(2,1)} fusion(bf16[32,128,2048]{2,1,0:T(8,128)(2,1)} %get-tuple-element.134, s32[1024]{0:T(1024)S(1)} %pad_clamp_fusion.3), kind=kCustom, calls=%fused_computation.clone.1 | custom fusion | bytes 33554560 | tf_op jit(solution)/shard_map/while/body/eval_jaxpr/gather | solution.py:45
  298.4 13.8 %bitcast_dynamic-update-slice_fusion.2 = f32[8,4,128,2048]{2,3,1,0:T(8,128)} fusion(f32[8,4,128,2048]{2,3,1,0:T(8,128)} %get-tuple-element.120, s32[]{:T(128)} %get-tuple-element.119, bf16[8,4,128,2048]{3,2,1,0:T(8,128)(2,1)} %bitcast.47, bf16[8,32,128,128]{3,2,1,0:T(8,128)(2,1)} %get-tuple-element.132, s32[]{:T(128)S(6)} %select_n.95), kind=kOutput, calls=%fused_computation.8.clone.1 | convolution fusion | flops 2147483648 | bytes 22020612 | tf_op jit(solution)/shard_map/while/body/eval_jaxpr/prxy,pryz->rxz/dot_general | solution.py:46
  312.1 0.6 dynamic_slice.19
  313.5 13.1 %gather_fusion = bf16[32,128,2048]{2,1,0:T(8,128)(2,1)} fusion(bf16[32,128,2048]{2,1,0:T(8,128)(2,1)} %get-tuple-element.134, s32[1024]{0:T(1024)S(1)} %pad_clamp_fusion.3), kind=kCustom, calls=%fused_computation.clone.1 | custom fusion | bytes 33554560 | tf_op jit(solution)/shard_map/while/body/eval_jaxpr/gather | solution.py:45
  326.7 13.8 %bitcast_dynamic-update-slice_fusion.2 = f32[8,4,128,2048]{2,3,1,0:T(8,128)} fusion(f32[8,4,128,2048]{2,3,1,0:T(8,128)} %get-tuple-element.120, s32[]{:T(128)} %get-tuple-element.119, bf16[8,4,128,2048]{3,2,1,0:T(8,128)(2,1)} %bitcast.47, bf16[8,32,128,128]{3,2,1,0:T(8,128)(2,1)} %get-tuple-element.132, s32[]{:T(128)S(6)} %select_n.95), kind=kOutput, calls=%fused_computation.8.clone.1 | convolution fusion | flops 2147483648 | bytes 22020612 | tf_op jit(solution)/shard_map/while/body/eval_jaxpr/prxy,pryz->rxz/dot_general | solution.py:46
  340.5 0.6 dynamic_slice.19
  341.9 13.1 %gather_fusion = bf16[32,128,2048]{2,1,0:T(8,128)(2,1)} fusion(bf16[32,128,2048]{2,1,0:T(8,128)(2,1)} %get-tuple-element.134, s32[1024]{0:T(1024)S(1)} %pad_clamp_fusion.3), kind=kCustom, calls=%fused_computation.clone.1 | custom fusion | bytes 33554560 | tf_op jit(solution)/shard_map/while/body/eval_jaxpr/gather | solution.py:45
  355.0 13.8 %bitcast_dynamic-update-slice_fusion.2 = f32[8,4,128,2048]{2,3,1,0:T(8,128)} fusion(f32[8,4,128,2048]{2,3,1,0:T(8,128)} %get-tuple-element.120, s32[]{:T(128)} %get-tuple-element.119, bf16[8,4,128,2048]{3,2,1,0:T(8,128)(2,1)} %bitcast.47, bf16[8,32,128,128]{3,2,1,0:T(8,128)(2,1)} %get-tuple-element.132, s32[]{:T(128)S(6)} %select_n.95), kind=kOutput, calls=%fused_computation.8.clone.1 | convolution fusion | flops 2147483648 | bytes 22020612 | tf_op jit(solution)/shard_map/while/body/eval_jaxpr/prxy,pryz->rxz/dot_general | solution.py:46
  368.9 0.6 dynamic_slice.19
  370.3 13.1 %gather_fusion = bf16[32,128,2048]{2,1,0:T(8,128)(2,1)} fusion(bf16[32,128,2048]{2,1,0:T(8,128)(2,1)} %get-tuple-element.134, s32[1024]{0:T(1024)S(1)} %pad_clamp_fusion.3), kind=kCustom, calls=%fused_computation.clone.1 | custom fusion | bytes 33554560 | tf_op jit(solution)/shard_map/while/body/eval_jaxpr/gather | solution.py:45
  383.4 13.8 %bitcast_dynamic-update-slice_fusion.2 = f32[8,4,128,2048]{2,3,1,0:T(8,128)} fusion(f32[8,4,128,2048]{2,3,1,0:T(8,128)} %get-tuple-element.120, s32[]{:T(128)} %get-tuple-element.119, bf16[8,4,128,2048]{3,2,1,0:T(8,128)(2,1)} %bitcast.47, bf16[8,32,128,128]{3,2,1,0:T(8,128)(2,1)} %get-tuple-element.132, s32[]{:T(128)S(6)} %select_n.95), kind=kOutput, calls=%fused_computation.8.clone.1 | convolution fusion | flops 2147483648 | bytes 22020612 | tf_op jit(solution)/shard_map/while/body/eval_jaxpr/prxy,pryz->rxz/dot_general | solution.py:46
  397.2 0.7 copy-done.1
  397.9 279.9 %reduce-scatter.2.cloned.1.call-done = f32[8,128,2048]{1,2,0:T(8,128)} async-done(((f32[32,128,2048]{1,2,0:T(8,128)}), f32[8,128,2048]{1,2,0:T(8,128)}) %reduce-scatter.2.cloned.1.call-update) | async-done | bytes 8388624 | tf_op jit(solution)/shard_map/reduce_scatter | solution.py:54
  677.8 9.1 %copy.22 = f32[8,128,16,128]{3,1,2,0:T(8,128)} copy(f32[8,128,16,128]{1,3,2,0:T(8,128)} %bitcast.50) | data formatting | bytes 16777216 | tf_op jit(solution)/shard_map/reshape | solution.py:55
  686.9 4.0 gather_fusion.1
  691.1 29.0 %psum.7 = f32[16,128]{1,0:T(8,128)S(1)} all-reduce(f32[16,128]{1,0:T(8,128)S(1)} %fusion.5), channel_id=1, replica_groups=mesh['row'=4,'col'=8,'layer'=4] {'row','layer'}, use_global_device_ids=true, to_apply=%region_7.8 | all-reduce | flops 2048 | bytes 16384 | tf_op jit(solution)/shard_map/psum | solution.py:63
  720.2 0.6 gather_fusion.2
  720.7 1.1 bitcast_multiply_fusion
  (51 shorter events, 2.4 us)
Async XLA Ops:
  6.5 51.1 %all-gather.5.cloned.1.call-start = ((), (), s32[]{:S(2)}) async-start(), calls=%async_computation.1 | async-start | bytes 5242880 | tf_op jit(solution)/shard_map/all_gather | solution.py:21
  7.3 163.2 %all-gather.7.cloned.1.call-start = ((), (), s32[]{:S(2)}) async-start(), calls=%async_computation.3 | async-start | bytes 9437184 | tf_op jit(solution)/shard_map/all_gather | solution.py:36
  11.8 1.0 copy-start
  12.8 665.0 %reduce-scatter.2.cloned.1.call-start = ((), (), s32[]{:S(2)}) async-start(), calls=%async_computation.2 | async-start | bytes 41943040 | tf_op jit(solution)/shard_map/reduce_scatter | solution.py:54
  397.2 0.7 copy-start.1
Sparse Core Ops, SparseCore 0:
  9.0 48.6 all-gather.4
  60.0 110.3 all-gather.6
  397.3 280.3 reduce-scatter.1
where the time goes:
time: 731 us; the launch traced here: 728 us
  waiting for transfers between devices  343 us (47%)
  local copies, waits for them, and re-layouts  205 us (28%)
  matrix products  111 us (15%)
  blocking collectives  48.2 us (7%)
  between operations  13.8 us (2%)
    reduce_scatter x1, waiting for transfers between devices, local(): lax.psum_scatter(partial_sum, 'layer', scatter_dimension=0, tiled=True)  280 us
    dot_general x8, matrix products, row_block(): jnp.einsum('prxy,pryz->rxz', left_block, right_block, preferred_element_t...  110 us
    gather x8, local copies, waits for them, and re-layouts, row_block(): right_block = graph_panel[index_block]  105 us
    scatter x2, local copies, waits for them, and re-layouts, local(): graph_panel = graph_panel.at[inner_rows, :, column_ids, :].set(flat_tiles)  43.6 us
    all_gather x1, waiting for transfers between devices, local(): lax.all_gather(ordered[None], 'col', axis=0, tiled=True)  40.7 us
    psum x1, blocking collectives, local(): column_total = lax.psum(local_mass, ('row', 'layer'))  29 us
    while x1, local copies, waits for them, and re-layouts, local(): lax.map(row_block, jnp.arange(rows_panel // RB, dtype=jnp.int32))  22.2 us
    all_gather x1, waiting for transfers between devices, local(): lax.all_gather(b_tiles, 'row', axis=0, tiled=True)  21.7 us
  transfers between devices with their start and end apart: 3, of which 3 were waited for; matrix products, arithmetic and copies ran while one was open for 11% of the time, Pallas kernels for 0%

commit v1 on v0

--- a/solution.py
+++ b/solution.py
@@ -5,6 +5,13 @@
 
 BLK = 4
 RB = 4
+
+
+def all_by_exchange(x, axis, dim):
+    size = lax.axis_size(axis)
+    blocks = jnp.stack([x for _ in range(size)])
+    blocks = lax.all_to_all(blocks, axis, split_axis=0, concat_axis=0)
+    return jnp.concatenate(blocks, axis=dim)
 
 
 def local(a_tiles, a_coords, b_tiles, b_coords, out_coords):
@@ -33,7 +40,7 @@
     ordered = jnp.zeros_like(a_tiles[0, 0, 0]).at[own_rows].set(a_tiles[0, 0, 0])
     ordered_inner = jnp.zeros_like(own_inner).at[own_rows].set(own_inner)
     flow_all, inner_all = (
-        lax.all_gather(ordered[None], "col", axis=0, tiled=True),
+        all_by_exchange(ordered[None], "col", 0),
         lax.all_gather(ordered_inner[None], "col", axis=0, tiled=True),
     )
     slab_index = jnp.arange(col_count, dtype=jnp.int32)[:, None] * a_span + inner_all

time: 731 us -> 789 us (1.079)
  blocking collectives: 48.2 us -> 157 us
  waiting for transfers between devices: 343 us -> 282 us
    all_gather x1, blocking collectives: 5.32 us -> 114 us  [local(): lax.all_gather(b_coords, 'row', axis=0, tiled=True)]
    all_gather x1 -> x0, waiting for transfers between devices: 40.7 us -> none  [local(): lax.all_gather(ordered[None], 'col', axis=0, tiled=True)]
    all_gather x1, waiting for transfers between devices: 21.7 us -> 0.01 us  [local(): lax.all_gather(b_tiles, 'row', axis=0, tiled=True)]
  transfers between devices with their start and end apart: 3 -> 3, of which waited for: 3 -> 1; matrix products, arithmetic and copies ran while one was open for 11% -> 9% of each run, Pallas kernels for 0% -> 0%
where the time goes in v1:
time: 789 us; the launch traced here: 787 us
  waiting for transfers between devices  282 us (36%)
  local copies, waits for them, and re-layouts  208 us (26%)
  blocking collectives  157 us (20%)
  matrix products  111 us (14%)
  between operations  14.1 us (2%)
  starting transfers between devices  7.94 us (1%)
    reduce_scatter x1, waiting for transfers between devices, local(): lax.psum_scatter(partial_sum, 'layer', scatter_dimension=0, tiled=True)  282 us
    all_gather x1, blocking collectives, local(): lax.all_gather(b_coords, 'row', axis=0, tiled=True)  114 us
    dot_general x8, matrix products, row_block(): jnp.einsum('prxy,pryz->rxz', left_block, right_block, preferred_element_t...  110 us
    gather x8, local copies, waits for them, and re-layouts, row_block(): right_block = graph_panel[index_block]  105 us
    scatter x2, local copies, waits for them, and re-layouts, local(): graph_panel = graph_panel.at[inner_rows, :, column_ids, :].set(flat_tiles)  43.3 us
    psum x1, blocking collectives, local(): column_total = lax.psum(local_mass, ('row', 'layer'))  29 us
    while x1, local copies, waits for them, and re-layouts, local(): lax.map(row_block, jnp.arange(rows_panel // RB, dtype=jnp.int32))  22.2 us
  transfers between devices with their start and end apart: 3, of which 1 were waited for; matrix products, arithmetic and copies ran while one was open for 9% of the time, Pallas kernels for 0%

profile of v1, /device:TPU:0, one launch (start us, length us, event | category | flops | bytes accessed | tf_op | source)
XLA Modules:
  0.0 786.8 jit_solution(3279142669488154325)
XLA Ops:
  6.5 0.8 fusion.8
  7.3 0.2 broadcast_in_dim.16
  7.5 3.6 scatter_fusion
  11.1 5.4 stack.3
  16.5 7.9 all-to-all-start
  24.4 0.7 all-gather.3.cloned.1.call-update
  25.2 113.9 %all_gather.10 = s32[4,1,1,32,2]{3,4,2,1,0:T(2,128)S(1)} all-gather(s32[1,1,1,32,2]{3,4,2,1,0:T(2,128)S(1)} %copy-done), channel_id=1, replica_groups=mesh['row'=4,'col'=8,'layer'=4] {'row'}, dimensions={0}, use_global_device_ids=true | all-gather | bytes 1280 | tf_op jit(solution)/shard_map/all_gather | solution.py:29
  139.5 0.7 scatter_custom_fusion.1
  140.2 0.6 dynamic-slice
  141.3 0.2 dynamic-update-slice
  141.6 13.6 %all-reduce = s32[256]{0:T(256)S(1)} all-reduce(s32[256]{0:T(256)S(1)} %dynamic-update-slice), channel_id=2, replica_groups=mesh['row'=4,'col'=8,'layer'=4] {'col'}, use_global_device_ids=true, to_apply=%add | all-reduce | flops 256 | bytes 2048
  155.3 6.3 broadcast_in_dim.18
  161.6 20.8 %scatter_fusion.1 = bf16[32,128,16,128]{3,1,2,0:T(8,128)(2,1)} fusion(bf16[32,128,16,128]{3,1,2,0:T(8,128)(2,1)} %broadcast_in_dim.18, s32[128]{0:T(128)S(1)} %fusion.13, bf16[128,128,128]{2,1,0:T(8,128)(2,1)} %bitcast.51), kind=kCustom, calls=%fused_computation.5 | custom fusion | bytes 12583936 | tf_op jit(solution)/shard_map/scatter | solution.py:36
  182.4 22.5 %copy.16 = bf16[32,128,16,128]{1,3,2,0:T(8,128)(2,1)} copy(bf16[32,128,16,128]{3,1,2,0:T(8,128)(2,1)} %scatter_fusion.1) | data formatting | bytes 33554432 | tf_op jit(solution)/shard_map/scatter | solution.py:36
  204.9 22.2 %copy.18 = bf16[32,128,2048]{2,1,0:T(8,128)(2,1)} copy(bf16[32,128,2048]{1,2,0:T(8,128)(2,1)} %bitcast.48) | data formatting | bytes 33554432 | tf_op jit(solution)/shard_map/while | solution.py:57
  227.1 226.6 %while.10 = (s32[]{:T(128)}, f32[8,4,128,2048]{2,3,1,0:T(8,128)}, s32[8]{0:T(128)S(1)}, bf16[8,32,128,128]{3,2,1,0:T(8,128)(2,1)}, s32[8,32]{1,0:T(8,128)S(1)}, ...) while((s32[]{:T(128)}, f32[8,4,128,2048]{2,3,1,0:T(8,128)}, ...), condition=%wide.region_4.5_spmd, body=%wide.region_3.4_spmd.sunk | while | flops 2147484672 | bytes 55580068 | solution.py:57
  227.1 0.6 dynamic_slice.19
  228.5 13.1 %gather_fusion = bf16[32,128,2048]{2,1,0:T(8,128)(2,1)} fusion(bf16[32,128,2048]{2,1,0:T(8,128)(2,1)} %get-tuple-element.134, s32[1024]{0:T(1024)S(1)} %pad_clamp_fusion.3), kind=kCustom, calls=%fused_computation.clone.1 | custom fusion | bytes 33554560 | tf_op jit(solution)/shard_map/while/body/eval_jaxpr/gather | solution.py:52
  241.6 13.8 %bitcast_dynamic-update-slice_fusion.2 = f32[8,4,128,2048]{2,3,1,0:T(8,128)} fusion(f32[8,4,128,2048]{2,3,1,0:T(8,128)} %get-tuple-element.120, s32[]{:T(128)} %get-tuple-element.119, bf16[8,4,128,2048]{3,2,1,0:T(8,128)(2,1)} %bitcast.47, bf16[8,32,128,128]{3,2,1,0:T(8,128)(2,1)} %get-tuple-element.132, s32[]{:T(128)S(6)} %select_n.95), kind=kOutput, calls=%fused_computation.8.clone.1 | convolution fusion | flops 2147483648 | bytes 22020612 | tf_op jit(solution)/shard_map/while/body/eval_jaxpr/prxy,pryz->rxz/dot_general | solution.py:53
  255.4 0.6 dynamic_slice.19
  256.8 13.1 %gather_fusion = bf16[32,128,2048]{2,1,0:T(8,128)(2,1)} fusion(bf16[32,128,2048]{2,1,0:T(8,128)(2,1)} %get-tuple-element.134, s32[1024]{0:T(1024)S(1)} %pad_clamp_fusion.3), kind=kCustom, calls=%fused_computation.clone.1 | custom fusion | bytes 33554560 | tf_op jit(solution)/shard_map/while/body/eval_jaxpr/gather | solution.py:52
  269.9 13.8 %bitcast_dynamic-update-slice_fusion.2 = f32[8,4,128,2048]{2,3,1,0:T(8,128)} fusion(f32[8,4,128,2048]{2,3,1,0:T(8,128)} %get-tuple-element.120, s32[]{:T(128)} %get-tuple-element.119, bf16[8,4,128,2048]{3,2,1,0:T(8,128)(2,1)} %bitcast.47, bf16[8,32,128,128]{3,2,1,0:T(8,128)(2,1)} %get-tuple-element.132, s32[]{:T(128)S(6)} %select_n.95), kind=kOutput, calls=%fused_computation.8.clone.1 | convolution fusion | flops 2147483648 | bytes 22020612 | tf_op jit(solution)/shard_map/while/body/eval_jaxpr/prxy,pryz->rxz/dot_general | solution.py:53
  283.8 0.6 dynamic_slice.19
  285.1 13.1 %gather_fusion = bf16[32,128,2048]{2,1,0:T(8,128)(2,1)} fusion(bf16[32,128,2048]{2,1,0:T(8,128)(2,1)} %get-tuple-element.134, s32[1024]{0:T(1024)S(1)} %pad_clamp_fusion.3), kind=kCustom, calls=%fused_computation.clone.1 | custom fusion | bytes 33554560 | tf_op jit(solution)/shard_map/while/body/eval_jaxpr/gather | solution.py:52
  298.3 13.8 %bitcast_dynamic-update-slice_fusion.2 = f32[8,4,128,2048]{2,3,1,0:T(8,128)} fusion(f32[8,4,128,2048]{2,3,1,0:T(8,128)} %get-tuple-element.120, s32[]{:T(128)} %get-tuple-element.119, bf16[8,4,128,2048]{3,2,1,0:T(8,128)(2,1)} %bitcast.47, bf16[8,32,128,128]{3,2,1,0:T(8,128)(2,1)} %get-tuple-element.132, s32[]{:T(128)S(6)} %select_n.95), kind=kOutput, calls=%fused_computation.8.clone.1 | convolution fusion | flops 2147483648 | bytes 22020612 | tf_op jit(solution)/shard_map/while/body/eval_jaxpr/prxy,pryz->rxz/dot_general | solution.py:53
  312.1 0.6 dynamic_slice.19
  313.5 13.1 %gather_fusion = bf16[32,128,2048]{2,1,0:T(8,128)(2,1)} fusion(bf16[32,128,2048]{2,1,0:T(8,128)(2,1)} %get-tuple-element.134, s32[1024]{0:T(1024)S(1)} %pad_clamp_fusion.3), kind=kCustom, calls=%fused_computation.clone.1 | custom fusion | bytes 33554560 | tf_op jit(solution)/shard_map/while/body/eval_jaxpr/gather | solution.py:52
  326.6 13.8 %bitcast_dynamic-update-slice_fusion.2 = f32[8,4,128,2048]{2,3,1,0:T(8,128)} fusion(f32[8,4,128,2048]{2,3,1,0:T(8,128)} %get-tuple-element.120, s32[]{:T(128)} %get-tuple-element.119, bf16[8,4,128,2048]{3,2,1,0:T(8,128)(2,1)} %bitcast.47, bf16[8,32,128,128]{3,2,1,0:T(8,128)(2,1)} %get-tuple-element.132, s32[]{:T(128)S(6)} %select_n.95), kind=kOutput, calls=%fused_computation.8.clone.1 | convolution fusion | flops 2147483648 | bytes 22020612 | tf_op jit(solution)/shard_map/while/body/eval_jaxpr/prxy,pryz->rxz/dot_general | solution.py:53
  340.4 0.6 dynamic_slice.19
  341.8 13.1 %gather_fusion = bf16[32,128,2048]{2,1,0:T(8,128)(2,1)} fusion(bf16[32,128,2048]{2,1,0:T(8,128)(2,1)} %get-tuple-element.134, s32[1024]{0:T(1024)S(1)} %pad_clamp_fusion.3), kind=kCustom, calls=%fused_computation.clone.1 | custom fusion | bytes 33554560 | tf_op jit(solution)/shard_map/while/body/eval_jaxpr/gather | solution.py:52
  355.0 13.8 %bitcast_dynamic-update-slice_fusion.2 = f32[8,4,128,2048]{2,3,1,0:T(8,128)} fusion(f32[8,4,128,2048]{2,3,1,0:T(8,128)} %get-tuple-element.120, s32[]{:T(128)} %get-tuple-element.119, bf16[8,4,128,2048]{3,2,1,0:T(8,128)(2,1)} %bitcast.47, bf16[8,32,128,128]{3,2,1,0:T(8,128)(2,1)} %get-tuple-element.132, s32[]{:T(128)S(6)} %select_n.95), kind=kOutput, calls=%fused_computation.8.clone.1 | convolution fusion | flops 2147483648 | bytes 22020612 | tf_op jit(solution)/shard_map/while/body/eval_jaxpr/prxy,pryz->rxz/dot_general | solution.py:53
  368.7 0.6 dynamic_slice.19
  370.1 13.1 %gather_fusion = bf16[32,128,2048]{2,1,0:T(8,128)(2,1)} fusion(bf16[32,128,2048]{2,1,0:T(8,128)(2,1)} %get-tuple-element.134, s32[1024]{0:T(1024)S(1)} %pad_clamp_fusion.3), kind=kCustom, calls=%fused_computation.clone.1 | custom fusion | bytes 33554560 | tf_op jit(solution)/shard_map/while/body/eval_jaxpr/gather | solution.py:52
  383.2 13.8 %bitcast_dynamic-update-slice_fusion.2 = f32[8,4,128,2048]{2,3,1,0:T(8,128)} fusion(f32[8,4,128,2048]{2,3,1,0:T(8,128)} %get-tuple-element.120, s32[]{:T(128)} %get-tuple-element.119, bf16[8,4,128,2048]{3,2,1,0:T(8,128)(2,1)} %bitcast.47, bf16[8,32,128,128]{3,2,1,0:T(8,128)(2,1)} %get-tuple-element.132, s32[]{:T(128)S(6)} %select_n.95), kind=kOutput, calls=%fused_computation.8.clone.1 | convolution fusion | flops 2147483648 | bytes 22020612 | tf_op jit(solution)/shard_map/while/body/eval_jaxpr/prxy,pryz->rxz/dot_general | solution.py:53
  397.1 0.6 dynamic_slice.19
  398.4 13.1 %gather_fusion = bf16[32,128,2048]{2,1,0:T(8,128)(2,1)} fusion(bf16[32,128,2048]{2,1,0:T(8,128)(2,1)} %get-tuple-element.134, s32[1024]{0:T(1024)S(1)} %pad_clamp_fusion.3), kind=kCustom, calls=%fused_computation.clone.1 | custom fusion | bytes 33554560 | tf_op jit(solution)/shard_map/while/body/eval_jaxpr/gather | solution.py:52
  411.6 13.8 %bitcast_dynamic-update-slice_fusion.2 = f32[8,4,128,2048]{2,3,1,0:T(8,128)} fusion(f32[8,4,128,2048]{2,3,1,0:T(8,128)} %get-tuple-element.120, s32[]{:T(128)} %get-tuple-element.119, bf16[8,4,128,2048]{3,2,1,0:T(8,128)(2,1)} %bitcast.47, bf16[8,32,128,128]{3,2,1,0:T(8,128)(2,1)} %get-tuple-element.132, s32[]{:T(128)S(6)} %select_n.95), kind=kOutput, calls=%fused_computation.8.clone.1 | convolution fusion | flops 2147483648 | bytes 22020612 | tf_op jit(solution)/shard_map/while/body/eval_jaxpr/prxy,pryz->rxz/dot_general | solution.py:53
  425.4 0.6 dynamic_slice.19
  426.8 13.1 %gather_fusion = bf16[32,128,2048]{2,1,0:T(8,128)(2,1)} fusion(bf16[32,128,2048]{2,1,0:T(8,128)(2,1)} %get-tuple-element.134, s32[1024]{0:T(1024)S(1)} %pad_clamp_fusion.3), kind=kCustom, calls=%fused_computation.clone.1 | custom fusion | bytes 33554560 | tf_op jit(solution)/shard_map/while/body/eval_jaxpr/gather | solution.py:52
  439.9 13.8 %bitcast_dynamic-update-slice_fusion.2 = f32[8,4,128,2048]{2,3,1,0:T(8,128)} fusion(f32[8,4,128,2048]{2,3,1,0:T(8,128)} %get-tuple-element.120, s32[]{:T(128)} %get-tuple-element.119, bf16[8,4,128,2048]{3,2,1,0:T(8,128)(2,1)} %bitcast.47, bf16[8,32,128,128]{3,2,1,0:T(8,128)(2,1)} %get-tuple-element.132, s32[]{:T(128)S(6)} %select_n.95), kind=kOutput, calls=%fused_computation.8.clone.1 | convolution fusion | flops 2147483648 | bytes 22020612 | tf_op jit(solution)/shard_map/while/body/eval_jaxpr/prxy,pryz->rxz/dot_general | solution.py:53
  453.7 0.7 copy-done.1
  454.4 281.5 %reduce-scatter.2.cloned.1.call-done = f32[8,128,2048]{1,2,0:T(8,128)} async-done(((f32[32,128,2048]{1,2,0:T(8,128)}), f32[8,128,2048]{1,2,0:T(8,128)}) %reduce-scatter.2.cloned.1.call-update) | async-done | bytes 8388624 | tf_op jit(solution)/shard_map/reduce_scatter | solution.py:61
  735.9 9.1 %copy.20 = f32[8,128,16,128]{3,1,2,0:T(8,128)} copy(f32[8,128,16,128]{1,3,2,0:T(8,128)} %bitcast.50) | data formatting | bytes 16777216 | tf_op jit(solution)/shard_map/reshape | solution.py:62
  745.1 4.0 gather_fusion.1
  749.2 0.1 fusion.5
  749.3 29.0 %psum.7 = f32[16,128]{1,0:T(8,128)S(1)} all-reduce(f32[16,128]{1,0:T(8,128)S(1)} %fusion.5), channel_id=1, replica_groups=mesh['row'=4,'col'=8,'layer'=4] {'row','layer'}, use_global_device_ids=true, to_apply=%region_7.8 | all-reduce | flops 2048 | bytes 16384 | tf_op jit(solution)/shard_map/psum | solution.py:70
  778.3 0.6 gather_fusion.2
  778.9 1.1 bitcast_multiply_fusion
  (55 shorter events, 2.1 us)
Async XLA Ops:
  6.5 133.6 %copy-start.3 = (u32[128]{0:T(128)S(1)}, u32[128]{0:T(128)}, u32[]{:S(2)}) copy-start(u32[128]{0:T(128)} %constant.75) | copy-start | bytes 1540
  6.5 132.9 %copy-start.2 = (s32[1,1,1,32,2]{3,4,2,1,0:T(2,128)S(1)}, s32[1,1,1,32,2]{3,4,2,1,0:T(2,128)}, u32[]{:S(2)}) copy-start(s32[1,1,1,32,2]{3,4,2,1,0:T(2,128)} %param.8) | copy-start | bytes 772
  6.5 18.7 %copy-start = (s32[1,1,1,32,2]{3,4,2,1,0:T(2,128)S(1)}, s32[1,1,1,32,2]{3,4,2,1,0:T(2,128)}, u32[]{:S(2)}) copy-start(s32[1,1,1,32,2]{3,4,2,1,0:T(2,128)} %param.10) | copy-start | bytes 772
  16.5 210.6 %all-to-all-start = ((bf16[8,1,32,128,128]{4,3,2,1,0:T(8,128)(2,1)}), bf16[8,1,32,128,128]{4,3,2,1,0:T(8,128)(2,1)}, u32[]{:S(2)}, u32[]{:S(2)}) async-start(bf16[8,1,32,128,128]{4,3,2,1,0:T(8,128)(2,1)} %stack.3), calls=%async_computation | async-start | bytes 16777216 | tf_op jit(solution)/shard_map/all_to_all | solution.py:13
  24.4 130.9 %all-gather.3.cloned.1.call-start = ((), (), s32[]{:S(2)}) async-start(), calls=%async_computation.2 | async-start | bytes 5242880 | tf_op jit(solution)/shard_map/all_gather | solution.py:28
  25.1 710.8 %reduce-scatter.2.cloned.1.call-start = ((), (), s32[]{:S(2)}) async-start(), calls=%async_computation.3 | async-start | bytes 41943040 | tf_op jit(solution)/shard_map/reduce_scatter | solution.py:61
  453.7 0.7 copy-start.1
Sparse Core Ops, SparseCore 0:
  26.9 123.0 all-gather.2
  453.9 282.0 reduce-scatter.1
